TPU v7x, 512 devices: a whole 4x4x16 slice. The times are simulated.
512 devices in a mesh: cand: 8 (over y, core), doc: 64 (over z, x).
Axes of the slice: x: 4, y: 4, z: 16, core: 2. Of those that a mesh axis runs over, the one named last changes fastest.
Arguments:
- queries: bfloat16 [8192, 8192], P('doc'), may hold values from -6 to 50
- keys_values: bfloat16 [2, 8192, 1024], P(None, 'doc', 'cand'), may hold values from -6 to 50
- factors: float32 [8, 64], P('cand'), may hold values from 1 to 16
- lengths: int32 [16], replicated, may hold values from 1 to 1024, 8192 in all
Outputs:
- attended: bfloat16 [8, 8192, 8192], P('cand', 'doc')
All inputs are finite; a program needn't handle non-finite values.
Results may differ from a plain program's by a relative error of at most 0.0053.
Values may be sent and summed in bfloat16 or wider, within the bound.
No kernel may reach another device: no remote copies, remote signals or barrier semaphores. Data moves between devices by JAX's collectives and lax.ppermute only.
A program may use at most 64 MiB of HBM per device.

v0:
```python
import math
import jax
import jax.numpy as jnp
from jax import lax
from jax.sharding import PartitionSpec as P

H = 64
KVH = 8
HD = 128
SPAN = 8
ROPE_BASE = 500000.0


def passed_along(value, axis, steps):
    count = lax.axis_size(axis)
    first, last = (max(0, -steps), min(count, count - steps))
    return lax.ppermute(value, axis, [(source, source + steps) for source in range(first, last)])


def locate(index_rows, lengths):
    ends = jnp.cumsum(lengths)
    starts = ends - lengths
    docid = jnp.sum((index_rows[:, None] >= ends[None, :]).astype(jnp.int32), axis=1)
    onehot = docid[:, None] == jnp.arange(lengths.shape[0], dtype=jnp.int32)[None, :]
    first_row = jnp.sum(jnp.where(onehot, starts[None, :], 0), axis=1)
    valid = index_rows >= 0
    return (jnp.where(valid, docid, -1), jnp.where(valid, index_rows - first_row, 0))


def rotate(values, offsets, factor):
    row_count = values.shape[0]
    heads_here = values.shape[1] // HD
    half_dim = HD // 2
    shaped = values.reshape(row_count, heads_here, HD).astype(jnp.float32)
    inverse = jnp.power(ROPE_BASE, -2.0 * jnp.arange(half_dim, dtype=jnp.float32) / HD) / factor
    angles = offsets.astype(jnp.float32)[:, None] * inverse[None, :]
    cosine = jnp.cos(angles)[:, None, :]
    sine = jnp.sin(angles)[:, None, :]
    first_half = shaped[..., :half_dim]
    second_half = shaped[..., half_dim:]
    turned = jnp.concatenate(
        [first_half * cosine - second_half * sine, second_half * cosine + first_half * sine],
        axis=-1,
    )
    return turned.reshape(row_count, heads_here * HD).astype(jnp.bfloat16)


def attend(query_rot, key_rot, value_rows, query_doc, query_index, key_doc, key_index):
    row_count = query_rot.shape[0]
    key_count = key_rot.shape[0]
    group_size = H // KVH
    q_grouped = query_rot.reshape(row_count, KVH, group_size, HD).transpose(1, 0, 2, 3)
    k_grouped = key_rot.reshape(key_count, KVH, HD).transpose(1, 0, 2)
    v_grouped = value_rows.reshape(key_count, KVH, HD).transpose(1, 0, 2)
    allowed = (
        (key_doc[None, :] == query_doc[:, None])
        & (key_index[None, :] <= query_index[:, None])
        & (key_doc[None, :] >= 0)
    )
    scale = 1.0 / math.sqrt(HD)

    def per_group(operands):
        q_part, k_part, v_part = operands
        scores = (
            jnp.einsum("rgd,wd->rgw", q_part, k_part, preferred_element_type=jnp.float32) * scale
        )
        scores = jnp.where(allowed[:, None, :], scores, -1e30)
        largest = jnp.max(scores, axis=-1, keepdims=True)
        expw = jnp.exp(scores - largest)
        total = jnp.sum(expw, axis=-1, keepdims=True)
        weights = expw.astype(jnp.bfloat16)
        numer = jnp.einsum("rgw,wd->rgd", weights, v_part, preferred_element_type=jnp.float32)
        return (numer / total).astype(jnp.bfloat16)

    mixed = lax.map(per_group, (q_grouped, k_grouped, v_grouped))
    return mixed.transpose(1, 0, 2, 3).reshape(row_count, H * HD)


def on_device(queries, keys_values, factors, lengths):
    row_count = queries.shape[0]
    device = lax.axis_index("doc")
    query_index = device * row_count + jnp.arange(row_count, dtype=jnp.int32)
    key_index = (device - SPAN) * row_count + jnp.arange((SPAN + 1) * row_count, dtype=jnp.int32)
    whole = lax.all_gather(keys_values, "cand", axis=2, tiled=True)
    pieces = []
    for distance in range(SPAN, 0, -1):
        pieces.append(passed_along(whole, "doc", distance))
    pieces.append(whole)
    window = jnp.concatenate(pieces, axis=1)
    query_doc, query_offset = locate(query_index, lengths)
    key_doc, key_offset = locate(key_index, lengths)
    factor = factors[0]
    query_rot = rotate(queries, query_offset, factor)
    key_rot = rotate(window[0], key_offset, factor)
    mixed = attend(query_rot, key_rot, window[1], query_doc, query_index, key_doc, key_index)
    return mixed[None]


def solution(mesh):
    placed = (P("doc", None), P(None, "doc", "cand"), P("cand", None), P())
    return jax.shard_map(
        on_device, mesh=mesh, in_specs=placed, out_specs=P("cand", "doc", None), check_vma=False
    )
```

profile of v0, /device:TPU:448, one launch (start us, length us, event | category | flops | bytes accessed | tf_op | source)
XLA Modules:
  0.0 222.4 jit_solution(7817300378528015322)
XLA Ops:
  1.0 13.6 %all_gather.3 = bf16[2,128,1024]{1,2,0:T(8,128)(2,1)S(1)} all-gather(bf16[2,128,128]{1,2,0:T(8,128)(2,1)S(1)} %copy.19), channel_id=1, replica_groups=mesh['cand'=8,'doc'=64] {'cand'}, dimensions={2}, use_global_device_ids=true | all-gather | bytes 589824 | tf_op jit(solution)/shard_map/all_gather | solution.py:84
  14.6 1.3 collective-permute-start
  15.9 5.1 %collective-permute-start.1 = (bf16[2,128,1024]{1,2,0:T(8,128)(2,1)S(1)}, bf16[2,128,1024]{1,2,0:T(8,128)(2,1)S(1)}, u32[]{:S(2)}, u32[]{:S(2)}) collective-permute-start(bf16[2,128,1024]{1,2,0:T(8,128)(2,1)S(1)} %all_gather.3), channel_id=1, source_target_pairs={{0,7},{1,8},{2,9},{3,10},{4,11},{5,12},{6,13},{7,14},{8,15},{9,16}... | collective-permute-start | bytes 1572872 | tf_op jit(solution)/shard_map/ppermute | solution.py:17
  21.0 1.9 collective-permute-start.2
  22.9 1.9 collective-permute-start.3
  24.9 1.9 collective-permute-start.4
  26.8 2.0 convert_bitcast_fusion
  29.6 4.6 %fusion.35 = (f32[128,64,64]{2,1,0:T(8,128)}, f32[128,64,64]{2,1,0:T(8,128)}) fusion(f32[128,64,128]{2,1,0:T(8,128)S(1)} %bitcast.48), kind=kLoop, calls=%fused_computation.60 | loop fusion | bytes 8388608 | tf_op jit(solution)/shard_map/slice | solution.py:39
  35.1 8.3 %subtract_convert_fusion = (bf16[128,64,64]{2,0,1:T(8,128)(2,1)S(1)}, bf16[128,64,64]{2,0,1:T(8,128)(2,1)S(1)}) fusion(f32[128,64,64]{2,1,0:T(8,128)} %get-tuple-element.116, f32[128,64,64]{2,1,0:T(8,128)} %get-tuple-element.115, f32[128,64]{1,0:T(8,128)S(1)} %get-tuple-element.120, f32[128,64]{1,0:T(8,128)S(1)} %get-tuple-element.119), kind=kLoop, calls=%fused_computation.23 | loop fusion | flops 4194304 | bytes 6356992 | tf_op jit(solution)/shard_map/convert.4
  43.5 1.1 multiply_cosine_fusion
  44.6 2.5 %pad_maximum_fusion = bf16[128,64,128]{2,0,1:T(8,128)(2,1)} fusion(bf16[128,64,64]{2,0,1:T(8,128)(2,1)S(1)} %get-tuple-element.110, bf16[128,64,64]{2,0,1:T(8,128)(2,1)S(1)} %get-tuple-element.109), kind=kLoop, calls=%fused_computation.27 | loop fusion | flops 4194304 | bytes 4194304 | tf_op jit(solution)/shard_map/concatenate | solution.py:41
  47.1 2.1 collective-permute-start.5
  49.2 1.1 constant_dynamic-update-slice_fusion.8
  50.3 16.4 %collective-permute-done.1 = bf16[2,128,1024]{1,2,0:T(8,128)(2,1)S(1)} collective-permute-done((bf16[2,128,1024]{1,2,0:T(8,128)(2,1)S(1)}, bf16[2,128,1024]{1,2,0:T(8,128)(2,1)S(1)}, u32[]{:S(2)}, u32[]{:S(2)}) %collective-permute-start.1) | collective-permute-done | bytes 524320 | tf_op jit(solution)/shard_map/ppermute | solution.py:17
  66.7 1.9 collective-permute-start.6
  68.8 22.0 %collective-permute-done.2 = bf16[2,128,1024]{1,2,0:T(8,128)(2,1)S(1)} collective-permute-done((bf16[2,128,1024]{1,2,0:T(8,128)(2,1)S(1)}, bf16[2,128,1024]{1,2,0:T(8,128)(2,1)S(1)}, u32[]{:S(2)}, u32[]{:S(2)}) %collective-permute-start.2) | collective-permute-done | bytes 524320 | tf_op jit(solution)/shard_map/ppermute | solution.py:17
  90.8 1.9 collective-permute-start.7
  92.9 20.1 %collective-permute-done.3 = bf16[2,128,1024]{1,2,0:T(8,128)(2,1)S(1)} collective-permute-done((bf16[2,128,1024]{1,2,0:T(8,128)(2,1)S(1)}, bf16[2,128,1024]{1,2,0:T(8,128)(2,1)S(1)}, u32[]{:S(2)}, u32[]{:S(2)}) %collective-permute-start.3) | collective-permute-done | bytes 524320 | tf_op jit(solution)/shard_map/ppermute | solution.py:17
  113.2 6.8 %collective-permute-done.5 = bf16[2,128,1024]{1,2,0:T(8,128)(2,1)S(1)} collective-permute-done((bf16[2,128,1024]{1,2,0:T(8,128)(2,1)S(1)}, bf16[2,128,1024]{1,2,0:T(8,128)(2,1)S(1)}, u32[]{:S(2)}, u32[]{:S(2)}) %collective-permute-start.5) | collective-permute-done | bytes 524320 | tf_op jit(solution)/shard_map/ppermute | solution.py:17
  120.1 14.6 %collective-permute-done.6 = bf16[2,128,1024]{1,2,0:T(8,128)(2,1)S(1)} collective-permute-done((bf16[2,128,1024]{1,2,0:T(8,128)(2,1)S(1)}, bf16[2,128,1024]{1,2,0:T(8,128)(2,1)S(1)}, u32[]{:S(2)}, u32[]{:S(2)}) %collective-permute-start.6) | collective-permute-done | bytes 524320 | tf_op jit(solution)/shard_map/ppermute | solution.py:17
  134.9 31.8 %collective-permute-done.7 = bf16[2,128,1024]{1,2,0:T(8,128)(2,1)S(1)} collective-permute-done((bf16[2,128,1024]{1,2,0:T(8,128)(2,1)S(1)}, bf16[2,128,1024]{1,2,0:T(8,128)(2,1)S(1)}, u32[]{:S(2)}, u32[]{:S(2)}) %collective-permute-start.7) | collective-permute-done | bytes 524320 | tf_op jit(solution)/shard_map/ppermute | solution.py:17
  166.9 1.8 fusion.34
  169.9 47.3 %while.11 = (s32[]{:T(128)}, bf16[8,128,8,128]{3,1,2,0:T(8,128)(2,1)}, bf16[8,128,8,128]{3,1,2,0:T(8,128)(2,1)}, bf16[8,1152,128]{1,2,0:T(8,128)(2,1)S(1)}, bf16...) while((s32[]{:T(128)}, ...), condition=%wide.region_8.9_spmd.clone, body=%wide.region_5.8_spmd.clone.sunk | while | flops 613087232 | bytes 15598837 | solution.py:75
  170.1 2.1 fusion.43
  172.2 1.0 fusion.44
  173.2 2.6 %fusion.45 = bf16[8,128,8,128]{3,1,2,0:T(8,128)(2,1)} fusion(bf16[8,128,8,128]{3,1,2,0:T(8,128)(2,1)} %get-tuple-element.200, s32[]{:T(128)S(6)} %copy.43, f32[128,8,1152]{2,0,1:T(8,128)S(1)} %get-tuple-element.186, f32[128,8]{0,1:T(8,128)S(1)} %get-tuple-element.187, bf16[8,1152,128]{1,2,0:T(8,128)(2,1)} %get-tuple-element.214, ...), kind=kOutput, calls=%fused_computation.11.clone.1 | convolution fusion | flops 304611328 | bytes 5284864 | tf_op jit(solution)/shard_map/while/body/eval_jaxpr/rgw,wd->rgd/dot_general | solution.py:72
  176.1 2.1 fusion.43
  178.1 1.0 fusion.44
  179.1 2.6 %fusion.45 = bf16[8,128,8,128]{3,1,2,0:T(8,128)(2,1)} fusion(bf16[8,128,8,128]{3,1,2,0:T(8,128)(2,1)} %get-tuple-element.200, s32[]{:T(128)S(6)} %copy.43, f32[128,8,1152]{2,0,1:T(8,128)S(1)} %get-tuple-element.186, f32[128,8]{0,1:T(8,128)S(1)} %get-tuple-element.187, bf16[8,1152,128]{1,2,0:T(8,128)(2,1)} %get-tuple-element.214, ...), kind=kOutput, calls=%fused_computation.11.clone.1 | convolution fusion | flops 304611328 | bytes 5284864 | tf_op jit(solution)/shard_map/while/body/eval_jaxpr/rgw,wd->rgd/dot_general | solution.py:72
  182.0 2.1 fusion.43
  184.0 1.0 fusion.44
  185.1 2.6 %fusion.45 = bf16[8,128,8,128]{3,1,2,0:T(8,128)(2,1)} fusion(bf16[8,128,8,128]{3,1,2,0:T(8,128)(2,1)} %get-tuple-element.200, s32[]{:T(128)S(6)} %copy.43, f32[128,8,1152]{2,0,1:T(8,128)S(1)} %get-tuple-element.186, f32[128,8]{0,1:T(8,128)S(1)} %get-tuple-element.187, bf16[8,1152,128]{1,2,0:T(8,128)(2,1)} %get-tuple-element.214, ...), kind=kOutput, calls=%fused_computation.11.clone.1 | convolution fusion | flops 304611328 | bytes 5284864 | tf_op jit(solution)/shard_map/while/body/eval_jaxpr/rgw,wd->rgd/dot_general | solution.py:72
  187.9 2.1 fusion.43
  190.0 1.0 fusion.44
  191.0 2.6 %fusion.45 = bf16[8,128,8,128]{3,1,2,0:T(8,128)(2,1)} fusion(bf16[8,128,8,128]{3,1,2,0:T(8,128)(2,1)} %get-tuple-element.200, s32[]{:T(128)S(6)} %copy.43, f32[128,8,1152]{2,0,1:T(8,128)S(1)} %get-tuple-element.186, f32[128,8]{0,1:T(8,128)S(1)} %get-tuple-element.187, bf16[8,1152,128]{1,2,0:T(8,128)(2,1)} %get-tuple-element.214, ...), kind=kOutput, calls=%fused_computation.11.clone.1 | convolution fusion | flops 304611328 | bytes 5284864 | tf_op jit(solution)/shard_map/while/body/eval_jaxpr/rgw,wd->rgd/dot_general | solution.py:72
  193.8 2.1 fusion.43
  196.9 2.6 %fusion.45 = bf16[8,128,8,128]{3,1,2,0:T(8,128)(2,1)} fusion(bf16[8,128,8,128]{3,1,2,0:T(8,128)(2,1)} %get-tuple-element.200, s32[]{:T(128)S(6)} %copy.43, f32[128,8,1152]{2,0,1:T(8,128)S(1)} %get-tuple-element.186, f32[128,8]{0,1:T(8,128)S(1)} %get-tuple-element.187, bf16[8,1152,128]{1,2,0:T(8,128)(2,1)} %get-tuple-element.214, ...), kind=kOutput, calls=%fused_computation.11.clone.1 | convolution fusion | flops 304611328 | bytes 5284864 | tf_op jit(solution)/shard_map/while/body/eval_jaxpr/rgw,wd->rgd/dot_general | solution.py:72
  199.7 2.1 fusion.43
  201.8 1.0 fusion.44
  202.8 2.6 %fusion.45 = bf16[8,128,8,128]{3,1,2,0:T(8,128)(2,1)} fusion(bf16[8,128,8,128]{3,1,2,0:T(8,128)(2,1)} %get-tuple-element.200, s32[]{:T(128)S(6)} %copy.43, f32[128,8,1152]{2,0,1:T(8,128)S(1)} %get-tuple-element.186, f32[128,8]{0,1:T(8,128)S(1)} %get-tuple-element.187, bf16[8,1152,128]{1,2,0:T(8,128)(2,1)} %get-tuple-element.214, ...), kind=kOutput, calls=%fused_computation.11.clone.1 | convolution fusion | flops 304611328 | bytes 5284864 | tf_op jit(solution)/shard_map/while/body/eval_jaxpr/rgw,wd->rgd/dot_general | solution.py:72
  205.6 2.1 fusion.43
  207.7 1.0 fusion.44
  208.7 2.6 %fusion.45 = bf16[8,128,8,128]{3,1,2,0:T(8,128)(2,1)} fusion(bf16[8,128,8,128]{3,1,2,0:T(8,128)(2,1)} %get-tuple-element.200, s32[]{:T(128)S(6)} %copy.43, f32[128,8,1152]{2,0,1:T(8,128)S(1)} %get-tuple-element.186, f32[128,8]{0,1:T(8,128)S(1)} %get-tuple-element.187, bf16[8,1152,128]{1,2,0:T(8,128)(2,1)} %get-tuple-element.214, ...), kind=kOutput, calls=%fused_computation.11.clone.1 | convolution fusion | flops 304611328 | bytes 5284864 | tf_op jit(solution)/shard_map/while/body/eval_jaxpr/rgw,wd->rgd/dot_general | solution.py:72
  211.5 2.1 fusion.43
  213.6 1.0 fusion.44
  214.6 2.6 %fusion.45 = bf16[8,128,8,128]{3,1,2,0:T(8,128)(2,1)} fusion(bf16[8,128,8,128]{3,1,2,0:T(8,128)(2,1)} %get-tuple-element.200, s32[]{:T(128)S(6)} %copy.43, f32[128,8,1152]{2,0,1:T(8,128)S(1)} %get-tuple-element.186, f32[128,8]{0,1:T(8,128)S(1)} %get-tuple-element.187, bf16[8,1152,128]{1,2,0:T(8,128)(2,1)} %get-tuple-element.214, ...), kind=kOutput, calls=%fused_computation.11.clone.1 | convolution fusion | flops 304611328 | bytes 5284864 | tf_op jit(solution)/shard_map/while/body/eval_jaxpr/rgw,wd->rgd/dot_general | solution.py:72
  217.2 2.9 %copy.22 = bf16[128,8,8,128]{3,2,1,0:T(8,128)(2,1)S(1)} copy(bf16[128,8,8,128]{3,0,2,1:T(8,128)(2,1)} %bitcast.52) | data formatting | bytes 4194304 | tf_op jit(solution)/shard_map/transpose | solution.py:76
  220.1 2.3 %broadcast_in_dim_reshape.3 = bf16[1,128,8192]{2,1,0:T(8,128)(2,1)} reshape(bf16[128,8,8,128]{3,2,1,0:T(8,128)(2,1)S(1)} %copy.22) | data formatting | bytes 4194304 | tf_op jit(solution)/shard_map/broadcast_in_dim;reshape | solution.py:96
  (44 shorter events, 7.5 us)
Async XLA Ops:
  14.6 32.5 %collective-permute-start = (bf16[2,128,1024]{1,2,0:T(8,128)(2,1)S(1)}, bf16[2,128,1024]{1,2,0:T(8,128)(2,1)}, u32[]{:S(2)}, u32[]{:S(2)}) collective-permute-start(bf16[2,128,1024]{1,2,0:T(8,128)(2,1)S(1)} %all_gather.3), channel_id=1, source_target_pairs={{0,8},{1,9},{2,10},{3,11},{4,12},{5,13},{6,14},{7,15},{8,16},{9,17... | collective-permute-start | bytes 1572872 | tf_op jit(solution)/shard_map/ppermute | solution.py:17
  15.9 50.9 %collective-permute-start.1 = (bf16[2,128,1024]{1,2,0:T(8,128)(2,1)S(1)}, bf16[2,128,1024]{1,2,0:T(8,128)(2,1)S(1)}, u32[]{:S(2)}, u32[]{:S(2)}) collective-permute-start(bf16[2,128,1024]{1,2,0:T(8,128)(2,1)S(1)} %all_gather.3), channel_id=1, source_target_pairs={{0,7},{1,8},{2,9},{3,10},{4,11},{5,12},{6,13},{7,14},{8,15},{9,16}... | collective-permute-start | bytes 1572872 | tf_op jit(solution)/shard_map/ppermute | solution.py:17
  21.0 69.8 %collective-permute-start.2 = (bf16[2,128,1024]{1,2,0:T(8,128)(2,1)S(1)}, bf16[2,128,1024]{1,2,0:T(8,128)(2,1)S(1)}, u32[]{:S(2)}, u32[]{:S(2)}) collective-permute-start(bf16[2,128,1024]{1,2,0:T(8,128)(2,1)S(1)} %all_gather.3), channel_id=1, source_target_pairs={{0,6},{1,7},{2,8},{3,9},{4,10},{5,11},{6,12},{7,13},{8,14},{9,15},... | collective-permute-start | bytes 1572872 | tf_op jit(solution)/shard_map/ppermute | solution.py:17
  22.9 90.0 %collective-permute-start.3 = (bf16[2,128,1024]{1,2,0:T(8,128)(2,1)S(1)}, bf16[2,128,1024]{1,2,0:T(8,128)(2,1)S(1)}, u32[]{:S(2)}, u32[]{:S(2)}) collective-permute-start(bf16[2,128,1024]{1,2,0:T(8,128)(2,1)S(1)} %all_gather.3), channel_id=1, source_target_pairs={{0,5},{1,6},{2,7},{3,8},{4,9},{5,10},{6,11},{7,12},{8,13},{9,14},{... | collective-permute-start | bytes 1572872 | tf_op jit(solution)/shard_map/ppermute | solution.py:17
  24.9 88.2 %collective-permute-start.4 = (bf16[2,128,1024]{1,2,0:T(8,128)(2,1)S(1)}, bf16[2,128,1024]{1,2,0:T(8,128)(2,1)S(1)}, u32[]{:S(2)}, u32[]{:S(2)}) collective-permute-start(bf16[2,128,1024]{1,2,0:T(8,128)(2,1)S(1)} %all_gather.3), channel_id=1, source_target_pairs={{0,4},{1,5},{2,6},{3,7},{4,8},{5,9},{6,10},{7,11},{8,12},{9,13},{1... | collective-permute-start | bytes 1572872 | tf_op jit(solution)/shard_map/ppermute | solution.py:17
  29.5 4.6 %copy-start.1 = (f32[1,64]{1,0:T(1,128)S(1)}, f32[1,64]{1,0:T(1,128)}, u32[]{:S(2)}) copy-start(f32[1,64]{1,0:T(1,128)} %param.8) | copy-start | bytes 772
  29.6 4.6 %copy-start = (s32[16]{0:T(128)S(1)}, s32[16]{0:T(128)}, u32[]{:S(2)}) copy-start(s32[16]{0:T(128)} %param.9) | copy-start | bytes 196
  47.1 72.9 %collective-permute-start.5 = (bf16[2,128,1024]{1,2,0:T(8,128)(2,1)S(1)}, bf16[2,128,1024]{1,2,0:T(8,128)(2,1)S(1)}, u32[]{:S(2)}, u32[]{:S(2)}) collective-permute-start(bf16[2,128,1024]{1,2,0:T(8,128)(2,1)S(1)} %all_gather.3), channel_id=1, source_target_pairs={{0,3},{1,4},{2,5},{3,6},{4,7},{5,8},{6,9},{7,10},{8,11},{9,12},{10... | collective-permute-start | bytes 1572872 | tf_op jit(solution)/shard_map/ppermute | solution.py:17
  66.7 68.0 %collective-permute-start.6 = (bf16[2,128,1024]{1,2,0:T(8,128)(2,1)S(1)}, bf16[2,128,1024]{1,2,0:T(8,128)(2,1)S(1)}, u32[]{:S(2)}, u32[]{:S(2)}) collective-permute-start(bf16[2,128,1024]{1,2,0:T(8,128)(2,1)S(1)} %all_gather.3), channel_id=1, source_target_pairs={{0,2},{1,3},{2,4},{3,5},{4,6},{5,7},{6,8},{7,9},{8,10},{9,11},{10,... | collective-permute-start | bytes 1572872 | tf_op jit(solution)/shard_map/ppermute | solution.py:17
  90.8 75.9 %collective-permute-start.7 = (bf16[2,128,1024]{1,2,0:T(8,128)(2,1)S(1)}, bf16[2,128,1024]{1,2,0:T(8,128)(2,1)S(1)}, u32[]{:S(2)}, u32[]{:S(2)}) collective-permute-start(bf16[2,128,1024]{1,2,0:T(8,128)(2,1)S(1)} %all_gather.3), channel_id=1, source_target_pairs={{0,1},{1,2},{2,3},{3,4},{4,5},{5,6},{6,7},{7,8},{8,9},{9,10},{10,1... | collective-permute-start | bytes 1572872 | tf_op jit(solution)/shard_map/ppermute | solution.py:17
where the time goes:
time: 223 us; the launch traced here: 222 us
  waiting for transfers between devices  112 us (50%)
  matrix products  37.5 us (17%)
  other arithmetic  25.7 us (12%)
  starting transfers between devices  18.1 us (8%)
  local copies, waits for them, and re-layouts  15.5 us (7%)
  blocking collectives  13.6 us (6%)
    ppermute x8, waiting for transfers between devices, passed_along(): lax.ppermute(value, axis, [(source, source + steps) for source in range(f...  112 us
    dot_general x8, matrix products, per_group(): jnp.einsum('rgw,wd->rgd', weights, v_part, preferred_element_type=jnp.flo...  20.8 us
    ppermute x8, starting transfers between devices, passed_along(): lax.ppermute(value, axis, [(source, source + steps) for source in range(f...  18.1 us
    dot_general x8, matrix products, per_group(): jnp.einsum('rgd,wd->rgw', q_part, k_part, preferred_element_type=jnp.floa...  16.7 us
    all_gather x1, blocking collectives, on_device(): whole = lax.all_gather(keys_values, 'cand', axis=2, tiled=True)  13.6 us
    another operation x4, other arithmetic  9.14 us
    reduce_sum x8, other arithmetic, per_group(): total = jnp.sum(expw, axis=-1, keepdims=True)  8.08 us
    slice x1, local copies, waits for them, and re-layouts, rotate(): first_half = shaped[..., :half_dim]  4.58 us
  transfers between devices with their start and end apart: 8, of which 6 were waited for; matrix products, arithmetic and copies ran while one was open for 10% of the time, Pallas kernels for 0%

commit v1 on v0

--- a/solution.py
+++ b/solution.py
@@ -81,7 +81,11 @@
     device = lax.axis_index("doc")
     query_index = device * row_count + jnp.arange(row_count, dtype=jnp.int32)
     key_index = (device - SPAN) * row_count + jnp.arange((SPAN + 1) * row_count, dtype=jnp.int32)
-    whole = lax.all_gather(keys_values, "cand", axis=2, tiled=True)
+    size = lax.axis_size("cand")
+    repeats = [size if d == 2 else 1 for d in range(keys_values.ndim)]
+    whole = lax.all_to_all(
+        jnp.tile(keys_values, repeats), "cand", split_axis=2, concat_axis=2, tiled=True
+    )
     pieces = []
     for distance in range(SPAN, 0, -1):
         pieces.append(passed_along(whole, "doc", distance))

time: 223 us -> 235 us (1.054)
  blocking collectives: 13.6 us -> 0 us
  waiting for transfers between devices: 112 us -> 121 us
  starting transfers between devices: 18.1 us -> 25.3 us
  local copies, waits for them, and re-layouts: 15.5 us -> 21.7 us
  other arithmetic: 25.7 us -> 28.5 us
    all_gather x1 -> x0, blocking collectives: 13.6 us -> none  [on_device(): whole = lax.all_gather(keys_values, 'cand', axis=2, tiled=True)]
    ppermute x8, waiting for transfers between devices: 112 us -> 121 us  [passed_along(): lax.ppermute(value, axis, [(source, source + steps) for source in range(f...]
    all_to_all x0 -> x1, starting transfers between devices: none -> 4.47 us  [on_device(): lax.all_to_all(jnp.tile(keys_values, repeats), 'cand', split_axis=2, conc...]
    unnamed x14, local copies, waits for them, and re-layouts: 3.71 us -> 7.88 us
    ppermute x8, starting transfers between devices: 18.1 us -> 20.9 us  [passed_along(): lax.ppermute(value, axis, [(source, source + steps) for source in range(f...]
  transfers between devices with their start and end apart: 8 -> 9, of which waited for: 6 -> 7; matrix products, arithmetic and copies ran while one was open for 10% -> 12% of each run, Pallas kernels for 0% -> 0%
where the time goes in v1:
time: 235 us; the launch traced here: 234 us
  waiting for transfers between devices  121 us (51%)
  matrix products  37.5 us (16%)
  other arithmetic  28.5 us (12%)
  starting transfers between devices  25.3 us (11%)
  local copies, waits for them, and re-layouts  21.7 us (9%)
    ppermute x8, waiting for transfers between devices, passed_along(): lax.ppermute(value, axis, [(source, source + steps) for source in range(f...  121 us
    ppermute x8, starting transfers between devices, passed_along(): lax.ppermute(value, axis, [(source, source + steps) for source in range(f...  20.9 us
    dot_general x8, matrix products, per_group(): jnp.einsum('rgw,wd->rgd', weights, v_part, preferred_element_type=jnp.flo...  20.8 us
    dot_general x8, matrix products, per_group(): jnp.einsum('rgd,wd->rgw', q_part, k_part, preferred_element_type=jnp.floa...  16.7 us
    another operation x4, other arithmetic  10.5 us
    reduce_sum x8, other arithmetic, per_group(): total = jnp.sum(expw, axis=-1, keepdims=True)  8.08 us
    unnamed x14, local copies, waits for them, and re-layouts  7.88 us
  transfers between devices with their start and end apart: 9, of which 7 were waited for; matrix products, arithmetic and copies ran while one was open for 12% of the time, Pallas kernels for 0%

profile of v1, /device:TPU:448, one launch (start us, length us, event | category | flops | bytes accessed | tf_op | source)
XLA Modules:
  0.0 234.0 jit_solution(4008718499883065123)
XLA Ops:
  1.0 1.1 tile.4
  2.1 4.5 %all-to-all-start = ((bf16[2,128,1024]{1,0,2:T(2,128)(2,1)}), bf16[2,128,1024]{1,0,2:T(2,128)(2,1)S(1)}, u32[]{:S(2)}, u32[]{:S(2)}) async-start(bf16[2,128,1024]{1,0,2:T(2,128)(2,1)} %bitcast.4), calls=%async_computation | async-start | bytes 1048576 | tf_op jit(solution)/shard_map/all_to_all | solution.py:86
  6.6 2.0 convert_bitcast_fusion
  9.3 4.6 %fusion.35 = (f32[128,64,64]{2,1,0:T(8,128)}, f32[128,64,64]{2,1,0:T(8,128)}) fusion(f32[128,64,128]{2,1,0:T(8,128)S(1)} %bitcast.49), kind=kLoop, calls=%fused_computation.60 | loop fusion | bytes 8388608 | tf_op jit(solution)/shard_map/slice | solution.py:39
  14.9 9.7 %subtract_convert_fusion = (bf16[128,64,64]{2,0,1:T(8,128)(2,1)S(1)}, bf16[128,64,64]{2,0,1:T(8,128)(2,1)}) fusion(f32[128,64,64]{2,1,0:T(8,128)} %get-tuple-element.126, f32[128,64,64]{2,1,0:T(8,128)} %get-tuple-element.125, f32[128,64]{1,0:T(8,128)S(1)} %get-tuple-element.130, f32[128,64]{1,0:T(8,128)S(1)} %get-tuple-element.129), kind=kLoop, calls=%fused_computation.23 | loop fusion | flops 4194304 | bytes 6356992 | tf_op jit(solution)/shard_map/convert.4
  25.4 1.3 collective-permute-start
  26.7 5.1 %collective-permute-start.1 = (bf16[2,128,1024]{1,2,0:T(8,128)(2,1)}, bf16[2,128,1024]{1,2,0:T(8,128)(2,1)}, u32[]{:S(2)}, u32[]{:S(2)}) collective-permute-start(bf16[2,128,1024]{1,2,0:T(8,128)(2,1)} %copy.36), channel_id=1, source_target_pairs={{0,7},{1,8},{2,9},{3,10},{4,11},{5,12},{6,13},{7,14},{8,15},{9,16}... | collective-permute-start | bytes 1572872 | tf_op jit(solution)/shard_map/ppermute | solution.py:17
  31.8 1.1 multiply_cosine_fusion
  32.9 1.9 collective-permute-start.2
  34.9 1.9 collective-permute-start.3
  36.8 1.9 collective-permute-start.4
  38.7 4.1 %pad_maximum_fusion = bf16[128,64,128]{2,0,1:T(8,128)(2,1)} fusion(bf16[128,64,64]{2,0,1:T(8,128)(2,1)} %get-tuple-element.120, bf16[128,64,64]{2,0,1:T(8,128)(2,1)S(1)} %get-tuple-element.119), kind=kLoop, calls=%fused_computation.27 | loop fusion | flops 4194304 | bytes 4194304 | tf_op jit(solution)/shard_map/concatenate | solution.py:41
  42.8 2.1 collective-permute-done
  44.9 4.7 %collective-permute-start.5 = (bf16[2,128,1024]{1,2,0:T(8,128)(2,1)}, bf16[2,128,1024]{1,2,0:T(8,128)(2,1)S(1)}, u32[]{:S(2)}, u32[]{:S(2)}) collective-permute-start(bf16[2,128,1024]{1,2,0:T(8,128)(2,1)} %copy.36), channel_id=1, source_target_pairs={{0,3},{1,4},{2,5},{3,6},{4,7},{5,8},{6,9},{7,10},{8,11},{9,12},{10... | collective-permute-start | bytes 1572872 | tf_op jit(solution)/shard_map/ppermute | solution.py:17
  49.6 1.1 constant_dynamic-update-slice_fusion.8
  50.7 27.1 %collective-permute-done.1 = bf16[2,128,1024]{1,2,0:T(8,128)(2,1)} collective-permute-done((bf16[2,128,1024]{1,2,0:T(8,128)(2,1)}, bf16[2,128,1024]{1,2,0:T(8,128)(2,1)}, u32[]{:S(2)}, u32[]{:S(2)}) %collective-permute-start.1) | collective-permute-done | bytes 524320 | tf_op jit(solution)/shard_map/ppermute | solution.py:17
  77.9 2.1 collective-permute-start.6
  80.0 1.2 constant_dynamic-update-slice_fusion.7
  81.2 20.7 %collective-permute-done.2 = bf16[2,128,1024]{1,2,0:T(8,128)(2,1)} collective-permute-done((bf16[2,128,1024]{1,2,0:T(8,128)(2,1)}, bf16[2,128,1024]{1,2,0:T(8,128)(2,1)}, u32[]{:S(2)}, u32[]{:S(2)}) %collective-permute-start.2) | collective-permute-done | bytes 524320 | tf_op jit(solution)/shard_map/ppermute | solution.py:17
  101.9 1.9 collective-permute-start.7
  103.8 1.2 constant_dynamic-update-slice_fusion.6
  105.0 19.1 %collective-permute-done.3 = bf16[2,128,1024]{1,2,0:T(8,128)(2,1)} collective-permute-done((bf16[2,128,1024]{1,2,0:T(8,128)(2,1)}, bf16[2,128,1024]{1,2,0:T(8,128)(2,1)}, u32[]{:S(2)}, u32[]{:S(2)}) %collective-permute-start.3) | collective-permute-done | bytes 524320 | tf_op jit(solution)/shard_map/ppermute | solution.py:17
  124.1 1.2 constant_dynamic-update-slice_fusion.5
  125.3 1.2 constant_dynamic-update-slice_fusion.4
  126.5 5.0 %collective-permute-done.5 = bf16[2,128,1024]{1,2,0:T(8,128)(2,1)S(1)} collective-permute-done((bf16[2,128,1024]{1,2,0:T(8,128)(2,1)}, bf16[2,128,1024]{1,2,0:T(8,128)(2,1)S(1)}, u32[]{:S(2)}, u32[]{:S(2)}) %collective-permute-start.5) | collective-permute-done | bytes 524320 | tf_op jit(solution)/shard_map/ppermute | solution.py:17
  131.5 14.4 %collective-permute-done.6 = bf16[2,128,1024]{1,2,0:T(8,128)(2,1)S(1)} collective-permute-done((bf16[2,128,1024]{1,2,0:T(8,128)(2,1)}, bf16[2,128,1024]{1,2,0:T(8,128)(2,1)S(1)}, u32[]{:S(2)}, u32[]{:S(2)}) %collective-permute-start.6) | collective-permute-done | bytes 524320 | tf_op jit(solution)/shard_map/ppermute | solution.py:17
  146.1 32.1 %collective-permute-done.7 = bf16[2,128,1024]{1,2,0:T(8,128)(2,1)S(1)} collective-permute-done((bf16[2,128,1024]{1,2,0:T(8,128)(2,1)}, bf16[2,128,1024]{1,2,0:T(8,128)(2,1)S(1)}, u32[]{:S(2)}, u32[]{:S(2)}) %collective-permute-start.7) | collective-permute-done | bytes 524320 | tf_op jit(solution)/shard_map/ppermute | solution.py:17
  178.5 1.8 fusion.34
  181.5 47.3 %while.11 = (s32[]{:T(128)}, bf16[8,128,8,128]{3,1,2,0:T(8,128)(2,1)}, bf16[8,128,8,128]{3,1,2,0:T(8,128)(2,1)}, bf16[8,1152,128]{1,2,0:T(8,128)(2,1)S(1)}, bf16...) while((s32[]{:T(128)}, ...), condition=%wide.region_8.9_spmd.clone, body=%wide.region_5.8_spmd.clone.sunk | while | flops 613087232 | bytes 15598837 | solution.py:75
  181.7 2.1 fusion.43
  184.8 2.6 %fusion.45 = bf16[8,128,8,128]{3,1,2,0:T(8,128)(2,1)} fusion(bf16[8,128,8,128]{3,1,2,0:T(8,128)(2,1)} %get-tuple-element.210, s32[]{:T(128)S(6)} %copy.69, f32[128,8,1152]{2,0,1:T(8,128)S(1)} %get-tuple-element.196, f32[128,8]{0,1:T(8,128)S(1)} %get-tuple-element.197, bf16[8,1152,128]{1,2,0:T(8,128)(2,1)} %get-tuple-element.224, ...), kind=kOutput, calls=%fused_computation.11.clone.1 | convolution fusion | flops 304611328 | bytes 5284864 | tf_op jit(solution)/shard_map/while/body/eval_jaxpr/rgw,wd->rgd/dot_general | solution.py:72
  187.6 2.1 fusion.43
  190.7 2.6 %fusion.45 = bf16[8,128,8,128]{3,1,2,0:T(8,128)(2,1)} fusion(bf16[8,128,8,128]{3,1,2,0:T(8,128)(2,1)} %get-tuple-element.210, s32[]{:T(128)S(6)} %copy.69, f32[128,8,1152]{2,0,1:T(8,128)S(1)} %get-tuple-element.196, f32[128,8]{0,1:T(8,128)S(1)} %get-tuple-element.197, bf16[8,1152,128]{1,2,0:T(8,128)(2,1)} %get-tuple-element.224, ...), kind=kOutput, calls=%fused_computation.11.clone.1 | convolution fusion | flops 304611328 | bytes 5284864 | tf_op jit(solution)/shard_map/while/body/eval_jaxpr/rgw,wd->rgd/dot_general | solution.py:72
  193.5 2.1 fusion.43
  195.6 1.0 fusion.44
  196.6 2.6 %fusion.45 = bf16[8,128,8,128]{3,1,2,0:T(8,128)(2,1)} fusion(bf16[8,128,8,128]{3,1,2,0:T(8,128)(2,1)} %get-tuple-element.210, s32[]{:T(128)S(6)} %copy.69, f32[128,8,1152]{2,0,1:T(8,128)S(1)} %get-tuple-element.196, f32[128,8]{0,1:T(8,128)S(1)} %get-tuple-element.197, bf16[8,1152,128]{1,2,0:T(8,128)(2,1)} %get-tuple-element.224, ...), kind=kOutput, calls=%fused_computation.11.clone.1 | convolution fusion | flops 304611328 | bytes 5284864 | tf_op jit(solution)/shard_map/while/body/eval_jaxpr/rgw,wd->rgd/dot_general | solution.py:72
  199.4 2.1 fusion.43
  202.5 2.6 %fusion.45 = bf16[8,128,8,128]{3,1,2,0:T(8,128)(2,1)} fusion(bf16[8,128,8,128]{3,1,2,0:T(8,128)(2,1)} %get-tuple-element.210, s32[]{:T(128)S(6)} %copy.69, f32[128,8,1152]{2,0,1:T(8,128)S(1)} %get-tuple-element.196, f32[128,8]{0,1:T(8,128)S(1)} %get-tuple-element.197, bf16[8,1152,128]{1,2,0:T(8,128)(2,1)} %get-tuple-element.224, ...), kind=kOutput, calls=%fused_computation.11.clone.1 | convolution fusion | flops 304611328 | bytes 5284864 | tf_op jit(solution)/shard_map/while/body/eval_jaxpr/rgw,wd->rgd/dot_general | solution.py:72
  205.3 2.1 fusion.43
  208.4 2.6 %fusion.45 = bf16[8,128,8,128]{3,1,2,0:T(8,128)(2,1)} fusion(bf16[8,128,8,128]{3,1,2,0:T(8,128)(2,1)} %get-tuple-element.210, s32[]{:T(128)S(6)} %copy.69, f32[128,8,1152]{2,0,1:T(8,128)S(1)} %get-tuple-element.196, f32[128,8]{0,1:T(8,128)S(1)} %get-tuple-element.197, bf16[8,1152,128]{1,2,0:T(8,128)(2,1)} %get-tuple-element.224, ...), kind=kOutput, calls=%fused_computation.11.clone.1 | convolution fusion | flops 304611328 | bytes 5284864 | tf_op jit(solution)/shard_map/while/body/eval_jaxpr/rgw,wd->rgd/dot_general | solution.py:72
  211.2 2.1 fusion.43
  214.3 2.6 %fusion.45 = bf16[8,128,8,128]{3,1,2,0:T(8,128)(2,1)} fusion(bf16[8,128,8,128]{3,1,2,0:T(8,128)(2,1)} %get-tuple-element.210, s32[]{:T(128)S(6)} %copy.69, f32[128,8,1152]{2,0,1:T(8,128)S(1)} %get-tuple-element.196, f32[128,8]{0,1:T(8,128)S(1)} %get-tuple-element.197, bf16[8,1152,128]{1,2,0:T(8,128)(2,1)} %get-tuple-element.224, ...), kind=kOutput, calls=%fused_computation.11.clone.1 | convolution fusion | flops 304611328 | bytes 5284864 | tf_op jit(solution)/shard_map/while/body/eval_jaxpr/rgw,wd->rgd/dot_general | solution.py:72
  217.1 2.1 fusion.43
  220.2 2.6 %fusion.45 = bf16[8,128,8,128]{3,1,2,0:T(8,128)(2,1)} fusion(bf16[8,128,8,128]{3,1,2,0:T(8,128)(2,1)} %get-tuple-element.210, s32[]{:T(128)S(6)} %copy.69, f32[128,8,1152]{2,0,1:T(8,128)S(1)} %get-tuple-element.196, f32[128,8]{0,1:T(8,128)S(1)} %get-tuple-element.197, bf16[8,1152,128]{1,2,0:T(8,128)(2,1)} %get-tuple-element.224, ...), kind=kOutput, calls=%fused_computation.11.clone.1 | convolution fusion | flops 304611328 | bytes 5284864 | tf_op jit(solution)/shard_map/while/body/eval_jaxpr/rgw,wd->rgd/dot_general | solution.py:72
  223.0 2.1 fusion.43
  226.1 2.6 %fusion.45 = bf16[8,128,8,128]{3,1,2,0:T(8,128)(2,1)} fusion(bf16[8,128,8,128]{3,1,2,0:T(8,128)(2,1)} %get-tuple-element.210, s32[]{:T(128)S(6)} %copy.69, f32[128,8,1152]{2,0,1:T(8,128)S(1)} %get-tuple-element.196, f32[128,8]{0,1:T(8,128)S(1)} %get-tuple-element.197, bf16[8,1152,128]{1,2,0:T(8,128)(2,1)} %get-tuple-element.224, ...), kind=kOutput, calls=%fused_computation.11.clone.1 | convolution fusion | flops 304611328 | bytes 5284864 | tf_op jit(solution)/shard_map/while/body/eval_jaxpr/rgw,wd->rgd/dot_general | solution.py:72
  228.7 2.9 %copy.47 = bf16[128,8,8,128]{3,2,1,0:T(8,128)(2,1)S(1)} copy(bf16[128,8,8,128]{3,0,2,1:T(8,128)(2,1)} %bitcast.53) | data formatting | bytes 4194304 | tf_op jit(solution)/shard_map/transpose | solution.py:76
  231.7 2.3 broadcast_in_dim_reshape.3
  (47 shorter events, 13.9 us)
Async XLA Ops:
  2.1 22.5 %all-to-all-start = ((bf16[2,128,1024]{1,0,2:T(2,128)(2,1)}), bf16[2,128,1024]{1,0,2:T(2,128)(2,1)S(1)}, u32[]{:S(2)}, u32[]{:S(2)}) async-start(bf16[2,128,1024]{1,0,2:T(2,128)(2,1)} %bitcast.4), calls=%async_computation | async-start | bytes 1048576 | tf_op jit(solution)/shard_map/all_to_all | solution.py:86
  9.3 4.6 %copy-start.1 = (f32[1,64]{1,0:T(1,128)S(1)}, f32[1,64]{1,0:T(1,128)}, u32[]{:S(2)}) copy-start(f32[1,64]{1,0:T(1,128)} %param.8) | copy-start | bytes 772
  9.3 4.6 %copy-start = (s32[16]{0:T(128)S(1)}, s32[16]{0:T(128)}, u32[]{:S(2)}) copy-start(s32[16]{0:T(128)} %param.9) | copy-start | bytes 196
  25.4 19.5 %collective-permute-start = (bf16[2,128,1024]{1,2,0:T(8,128)(2,1)}, bf16[2,128,1024]{1,2,0:T(8,128)(2,1)}, u32[]{:S(2)}, u32[]{:S(2)}) collective-permute-start(bf16[2,128,1024]{1,2,0:T(8,128)(2,1)} %copy.36), channel_id=1, source_target_pairs={{0,8},{1,9},{2,10},{3,11},{4,12},{5,13},{6,14},{7,15},{8,16},{9,17... | collective-permute-start | bytes 1572872 | tf_op jit(solution)/shard_map/ppermute | solution.py:17
  26.7 51.2 %collective-permute-start.1 = (bf16[2,128,1024]{1,2,0:T(8,128)(2,1)}, bf16[2,128,1024]{1,2,0:T(8,128)(2,1)}, u32[]{:S(2)}, u32[]{:S(2)}) collective-permute-start(bf16[2,128,1024]{1,2,0:T(8,128)(2,1)} %copy.36), channel_id=1, source_target_pairs={{0,7},{1,8},{2,9},{3,10},{4,11},{5,12},{6,13},{7,14},{8,15},{9,16}... | collective-permute-start | bytes 1572872 | tf_op jit(solution)/shard_map/ppermute | solution.py:17
  32.9 69.0 %collective-permute-start.2 = (bf16[2,128,1024]{1,2,0:T(8,128)(2,1)}, bf16[2,128,1024]{1,2,0:T(8,128)(2,1)}, u32[]{:S(2)}, u32[]{:S(2)}) collective-permute-start(bf16[2,128,1024]{1,2,0:T(8,128)(2,1)} %copy.36), channel_id=1, source_target_pairs={{0,6},{1,7},{2,8},{3,9},{4,10},{5,11},{6,12},{7,13},{8,14},{9,15},... | collective-permute-start | bytes 1572872 | tf_op jit(solution)/shard_map/ppermute | solution.py:17
  34.9 89.2 %collective-permute-start.3 = (bf16[2,128,1024]{1,2,0:T(8,128)(2,1)}, bf16[2,128,1024]{1,2,0:T(8,128)(2,1)}, u32[]{:S(2)}, u32[]{:S(2)}) collective-permute-start(bf16[2,128,1024]{1,2,0:T(8,128)(2,1)} %copy.36), channel_id=1, source_target_pairs={{0,5},{1,6},{2,7},{3,8},{4,9},{5,10},{6,11},{7,12},{8,13},{9,14},{... | collective-permute-start | bytes 1572872 | tf_op jit(solution)/shard_map/ppermute | solution.py:17
  36.8 88.5 %collective-permute-start.4 = (bf16[2,128,1024]{1,2,0:T(8,128)(2,1)}, bf16[2,128,1024]{1,2,0:T(8,128)(2,1)}, u32[]{:S(2)}, u32[]{:S(2)}) collective-permute-start(bf16[2,128,1024]{1,2,0:T(8,128)(2,1)} %copy.36), channel_id=1, source_target_pairs={{0,4},{1,5},{2,6},{3,7},{4,8},{5,9},{6,10},{7,11},{8,12},{9,13},{1... | collective-permute-start | bytes 1572872 | tf_op jit(solution)/shard_map/ppermute | solution.py:17
  44.9 86.5 %collective-permute-start.5 = (bf16[2,128,1024]{1,2,0:T(8,128)(2,1)}, bf16[2,128,1024]{1,2,0:T(8,128)(2,1)S(1)}, u32[]{:S(2)}, u32[]{:S(2)}) collective-permute-start(bf16[2,128,1024]{1,2,0:T(8,128)(2,1)} %copy.36), channel_id=1, source_target_pairs={{0,3},{1,4},{2,5},{3,6},{4,7},{5,8},{6,9},{7,10},{8,11},{9,12},{10... | collective-permute-start | bytes 1572872 | tf_op jit(solution)/shard_map/ppermute | solution.py:17
  77.9 68.1 %collective-permute-start.6 = (bf16[2,128,1024]{1,2,0:T(8,128)(2,1)}, bf16[2,128,1024]{1,2,0:T(8,128)(2,1)S(1)}, u32[]{:S(2)}, u32[]{:S(2)}) collective-permute-start(bf16[2,128,1024]{1,2,0:T(8,128)(2,1)} %copy.36), channel_id=1, source_target_pairs={{0,2},{1,3},{2,4},{3,5},{4,6},{5,7},{6,8},{7,9},{8,10},{9,11},{10,... | collective-permute-start | bytes 1572872 | tf_op jit(solution)/shard_map/ppermute | solution.py:17
  101.9 76.3 %collective-permute-start.7 = (bf16[2,128,1024]{1,2,0:T(8,128)(2,1)}, bf16[2,128,1024]{1,2,0:T(8,128)(2,1)S(1)}, u32[]{:S(2)}, u32[]{:S(2)}) collective-permute-start(bf16[2,128,1024]{1,2,0:T(8,128)(2,1)} %copy.36), channel_id=1, source_target_pairs={{0,1},{1,2},{2,3},{3,4},{4,5},{5,6},{6,7},{7,8},{8,9},{9,10},{10,1... | collective-permute-start | bytes 1572872 | tf_op jit(solution)/shard_map/ppermute | solution.py:17
